TPU v7x, 1024 devices: a whole 4x8x16 slice. The times are simulated.
1024 devices in a mesh: grid: 16 (over z_lo, core), patch: 32 (over x, y), cross: 2 (over z_hi).
Axes of the slice: x: 4, y: 8, z: 16 (z_hi: 2, z_lo: 8; z = z_hi * 8 + z_lo), core: 2. Of those that a mesh axis runs over, the one named last changes fastest.
Arguments:
- adjoint_now: float32 [3, 16, 256, 16, 128], P(None, 'grid', 'patch', 'cross'), may hold values from -6 to 6
- adjoint_prev: float32 [3, 16, 256, 16, 128], P(None, 'grid', 'patch', 'cross'), may hold values from -6 to 6
- stiffness: float32 [16, 256, 16, 128], P('grid', 'patch', 'cross'), may hold values from 0.08 to 0.3
- adjoint_source: bfloat16 [2, 3, 16, 256, 16, 128], P(None, None, 'grid', 'patch', 'cross'), may hold values from -6 to 6
- forward_field: bfloat16 [2, 3, 16, 256, 16, 128], P(None, None, 'grid', 'patch', 'cross'), may hold values from -6 to 6
- material_mask: int32 [16, 32, 2], P('grid', 'patch', 'cross'), may hold values 0 or 1
- interface_map: int32 [16, 256, 16], P('grid', 'patch', 'cross'), may hold values from 0 to 63, as said below
Outputs:
- adjoint_final: float32 [3, 16, 256, 16, 128], P(None, 'grid', 'patch', 'cross')
- kernel: float32 [16, 256, 16, 128], P('grid', 'patch', 'cross')
Inputs may be any that keep to these rules, and one draw needn't show every extreme that they name: `interface_map`: each value indexes a column of the same patch's plane of 8 x 8 cells, row-major, at most one cell away from the cell's own position along each horizontal dimension; the first and last cells of each patch are fed by their own column.
All inputs are finite; a program needn't handle non-finite values. No bound on the sum of `material_mask` on one device may be relied on, other than what follows from the above.
Results may differ from a plain program's by a relative error of at most 0.00035.
Values sent between devices are 32-bit elements; how exact they have to be, the bound alone decides.
No kernel may reach another device: no remote copies, remote signals or barrier semaphores. Data moves between devices by JAX's collectives and lax.ppermute only.
A program may use at most 32 MiB of HBM per device.

v0:
```python
import jax
import jax.numpy as jnp
from jax import lax
from jax.sharding import PartitionSpec as P

STEPS = 2


def with_halo(value, sides, width):
    for axis, dim in sides:
        peers, length = (lax.axis_size(axis), value.shape[dim])
        up = [(i, (i + 1) % peers) for i in range(peers)]
        down = [(j, i) for i, j in up]
        last = lax.slice_in_dim(value, length - width, length, axis=dim)
        initial = lax.slice_in_dim(value, 0, width, axis=dim)
        before = lax.ppermute(last, axis, up)
        after = lax.ppermute(initial, axis, down)
        value = jnp.concatenate([before, value, after], axis=dim)
    return value


def shifted(value, axis, by):
    peers = lax.axis_size(axis)
    pairs = [(i, i + by) for i in range(peers) if 0 <= i + by < peers]
    return lax.ppermute(value, axis, pairs)


def side_sums(field):
    padded = with_halo(field, (("patch", 2), ("cross", 3)), 1)
    total = padded[:, :, 2:, 1:-1] + padded[:, :, :-2, 1:-1]
    total = total + padded[:, :, 1:-1, 2:] + padded[:, :, 1:-1, :-2]
    return total


def local(
    adjoint_now,
    adjoint_prev,
    stiffness,
    adjoint_source,
    forward_field,
    material_mask,
    interface_map,
):
    rows = adjoint_now.shape[2]
    cols = adjoint_now.shape[3]
    flat_map = interface_map.reshape(-1)
    is_top = lax.axis_index("grid") == 0
    patch_mask = material_mask[0, 0, 0].astype(jnp.float32)
    field = adjoint_now
    older = adjoint_prev
    kernel = jnp.zeros(stiffness.shape, jnp.float32)
    for step in range(STEPS):
        slot = STEPS - 1 - step
        bottom = field[:, :, :, :, -1]
        from_above = shifted(bottom, "grid", 1)
        from_below = shifted(field[:, :, :, :, 0], "grid", -1)
        gathered = jnp.take(from_above.reshape(3, rows * cols), flat_map, axis=1).reshape(
            3, 1, rows, cols
        )
        top_plane = jnp.where(is_top, field[:, :, :, :, 0], gathered)
        upper = jnp.concatenate([top_plane[..., None], field[..., :-1]], axis=4)
        lower = jnp.concatenate([field[..., 1:], from_below[..., None]], axis=4)
        lap = side_sums(field) + upper + lower - 6.0 * field
        fresh = (
            2.0 * field - older + stiffness * lap + adjoint_source[slot].astype(jnp.float32)
        ) * patch_mask
        kernel = kernel + jnp.sum(fresh * forward_field[slot].astype(jnp.float32), axis=0)
        older = field
        field = fresh
    return (field, kernel)


def solution(mesh):
    in_specs = (
        P(None, "grid", "patch", "cross", None),
        P(None, "grid", "patch", "cross", None),
        P("grid", "patch", "cross", None),
        P(None, None, "grid", "patch", "cross", None),
        P(None, None, "grid", "patch", "cross", None),
        P("grid", "patch", "cross"),
        P("grid", "patch", "cross"),
    )
    out_specs = (P(None, "grid", "patch", "cross", None), P("grid", "patch", "cross", None))
    return jax.shard_map(local, mesh=mesh, in_specs=in_specs, out_specs=out_specs, check_vma=False)
```

profile of v0, /device:TPU:1, one launch (start us, length us, event | category | flops | bytes accessed | tf_op | source)
XLA Modules:
  0.0 89.1 jit_solution(14389857782653342525)
XLA Ops:
  0.6 0.7 fusion.27
  1.4 8.1 %collective-permute-start = (f32[3,1,1,8,128]{4,3,2,1,0:T(8,128)S(1)}, f32[3,1,1,8,128]{4,3,2,1,0:T(8,128)S(1)}, u32[]{:S(2)}, u32[]{:S(2)}) collective-permute-start(f32[3,1,1,8,128]{4,3,2,1,0:T(8,128)S(1)} %get-tuple-element.30), channel_id=1, source_target_pairs={{2,0},{4,2},{6,4},{8,6},{10,8},{12,10},{14,12},{16,14},{18,16},{20... | collective-permute-start | bytes 36872 | tf_op jit(solution)/shard_map/ppermute | solution.py:17
  9.5 1.9 %collective-permute-start.1 = (f32[3,1,1,8,128]{4,3,2,1,0:T(8,128)S(1)}, f32[3,1,1,8,128]{4,3,2,1,0:T(8,128)S(1)}, u32[]{:S(2)}, u32[]{:S(2)}) collective-permute-start(f32[3,1,1,8,128]{4,3,2,1,0:T(8,128)S(1)} %get-tuple-element.31), channel_id=1, source_target_pairs={{0,2},{2,4},{4,6},{6,8},{8,10},{10,12},{12,14},{14,16},{16,18},{18... | collective-permute-start | bytes 36872 | tf_op jit(solution)/shard_map/ppermute | solution.py:16
  11.4 1.0 %slice.103 = f32[3,1,8,8,1]{4,3,2,1,0:T(8,128)S(1)} slice(f32[3,1,8,8,128]{4,3,2,1,0:T(8,128)} %param.9), slice={[0:3], [0:1], [0:8], [0:8], [127:128]} | slice | bytes 1536 | tf_op jit(solution)/shard_map/slice | solution.py:54
  12.4 0.0 copy-start.5
  12.4 0.2 copy.184
  12.6 4.8 %collective-permute-start.4 = (f32[3,1,8,8]{3,2,0,1:T(8,128)S(1)}, f32[3,1,8,8]{3,2,0,1:T(8,128)S(1)}, u32[]{:S(2)}, u32[]{:S(2)}) collective-permute-start(f32[3,1,8,8]{3,2,0,1:T(8,128)S(1)} %bitcast.55), channel_id=1, source_target_pairs={{0,64},{64,128},{128,192},{192,256},{256,320},{320,384},{384,448},... | collective-permute-start | bytes 2312 | tf_op jit(solution)/shard_map/ppermute | solution.py:25
  17.4 0.0 copy-done.5
  17.5 0.1 reshape.112
  17.6 6.9 %collective-permute-done.4 = f32[3,1,8,8]{3,2,0,1:T(8,128)S(1)} collective-permute-done((f32[3,1,8,8]{3,2,0,1:T(8,128)S(1)}, f32[3,1,8,8]{3,2,0,1:T(8,128)S(1)}, u32[]{:S(2)}, u32[]{:S(2)}) %collective-permute-start.4) | collective-permute-done | bytes 800 | tf_op jit(solution)/shard_map/ppermute | solution.py:25
  24.5 0.1 copy.163
  24.6 0.6 gather_fusion
  25.2 0.0 copy-start
  25.2 0.1 select_bitcast_fusion.1
  25.3 0.5 copy.165
  25.8 0.3 copy-done
  26.1 0.1 slice_reduce_fusion.2
  26.2 2.1 %collective-permute-start.5 = (f32[3,1,8,8]{3,2,0,1:T(8,128)S(1)}, f32[3,1,8,8]{3,2,0,1:T(8,128)S(1)}, u32[]{:S(2)}, u32[]{:S(2)}) collective-permute-start(f32[3,1,8,8]{3,2,0,1:T(8,128)S(1)} %bitcast.50), channel_id=1, source_target_pairs={{64,0},{128,64},{192,128},{256,192},{320,256},{384,320},{448,384},... | collective-permute-start | bytes 2312 | tf_op jit(solution)/shard_map/ppermute | solution.py:25
  28.3 0.0 collective-permute-done.1
  28.3 0.0 collective-permute-done
  28.4 11.8 %collective-permute-start.2 = (f32[3,1,10,1,128]{4,3,2,1,0:T(1,128)S(1)}, f32[3,1,10,1,128]{4,3,2,1,0:T(1,128)S(1)}, u32[]{:S(2)}, u32[]{:S(2)}) collective-permute-start(f32[3,1,10,1,128]{4,3,2,1,0:T(1,128)S(1)} %get-tuple-element.20), channel_id=1, source_target_pairs={{1,0},{0,1},{3,2},{2,3},{5,4},{4,5},{7,6},{6,7},{9,8},{8,9},{11,10... | collective-permute-start | bytes 46088 | tf_op jit(solution)/shard_map/ppermute | solution.py:17
  40.2 2.2 %collective-permute-start.3 = (f32[3,1,10,1,128]{4,3,2,1,0:T(1,128)S(1)}, f32[3,1,10,1,128]{4,3,2,1,0:T(1,128)S(1)}, u32[]{:S(2)}, u32[]{:S(2)}) collective-permute-start(f32[3,1,10,1,128]{4,3,2,1,0:T(1,128)S(1)} %get-tuple-element.21), channel_id=1, source_target_pairs={{0,1},{1,0},{2,3},{3,2},{4,5},{5,4},{6,7},{7,6},{8,9},{9,8},{10,11... | collective-permute-start | bytes 46088 | tf_op jit(solution)/shard_map/ppermute | solution.py:16
  42.4 0.0 copy-start.2
  42.4 0.0 copy-start.3
  42.4 0.1 fusion.26
  43.1 0.0 collective-permute-done.5
  43.1 0.0 copy-start.1
  43.2 0.2 copy.166
  43.4 0.0 collective-permute-done.2
  43.4 10.1 %collective-permute-done.3 = f32[3,1,10,1,128]{4,3,2,1,0:T(1,128)S(1)} collective-permute-done((f32[3,1,10,1,128]{4,3,2,1,0:T(1,128)S(1)}, f32[3,1,10,1,128]{4,3,2,1,0:T(1,128)S(1)}, u32[]{:S(2)}, u32[]{:S(2)}) %collective-permute-start.3) | collective-permute-done | bytes 15392 | tf_op jit(solution)/shard_map/ppermute | solution.py:16
  53.5 0.0 copy-done.2
  53.5 0.0 copy-done.3
  53.5 0.0 copy-done.1
  53.5 0.1 fusion.17
  53.7 0.2 slice_reduce_fusion.1
  53.8 0.1 fusion.25
  53.9 5.5 %collective-permute-start.10 = (f32[3,1,8,8]{3,2,0,1:T(8,128)S(1)}, f32[3,1,8,8]{3,2,0,1:T(8,128)S(1)}, u32[]{:S(2)}, u32[]{:S(2)}) collective-permute-start(f32[3,1,8,8]{3,2,0,1:T(8,128)S(1)} %bitcast.54), channel_id=1, source_target_pairs={{0,64},{64,128},{128,192},{192,256},{256,320},{320,384},{384,448},... | collective-permute-start | bytes 2312 | tf_op jit(solution)/shard_map/ppermute | solution.py:25
  59.4 1.9 %collective-permute-start.7 = (f32[3,1,1,8,128]{4,3,2,1,0:T(8,128)S(1)}, f32[3,1,1,8,128]{4,3,2,1,0:T(8,128)S(1)}, u32[]{:S(2)}, u32[]{:S(2)}) collective-permute-start(f32[3,1,1,8,128]{4,3,2,1,0:T(8,128)S(1)} %get-tuple-element.22), channel_id=1, source_target_pairs={{0,2},{2,4},{4,6},{6,8},{8,10},{10,12},{12,14},{14,16},{16,18},{18... | collective-permute-start | bytes 36872 | tf_op jit(solution)/shard_map/ppermute | solution.py:16
  61.4 7.0 %collective-permute-start.6 = (f32[3,1,1,8,128]{4,3,2,1,0:T(8,128)S(1)}, f32[3,1,1,8,128]{4,3,2,1,0:T(8,128)S(1)}, u32[]{:S(2)}, u32[]{:S(2)}) collective-permute-start(f32[3,1,1,8,128]{4,3,2,1,0:T(8,128)S(1)} %get-tuple-element.23), channel_id=1, source_target_pairs={{2,0},{4,2},{6,4},{8,6},{10,8},{12,10},{14,12},{16,14},{18,16},{20... | collective-permute-start | bytes 36872 | tf_op jit(solution)/shard_map/ppermute | solution.py:17
  68.3 1.9 %collective-permute-start.11 = (f32[3,1,8,8]{3,2,0,1:T(8,128)S(1)}, f32[3,1,8,8]{3,2,0,1:T(8,128)S(1)}, u32[]{:S(2)}, u32[]{:S(2)}) collective-permute-start(f32[3,1,8,8]{3,2,0,1:T(8,128)S(1)} %bitcast.51), channel_id=1, source_target_pairs={{64,0},{128,64},{192,128},{256,192},{320,256},{384,320},{448,384},... | collective-permute-start | bytes 2312 | tf_op jit(solution)/shard_map/ppermute | solution.py:25
  70.3 0.0 collective-permute-done.10
  70.3 0.1 copy.168
  70.4 0.6 gather_fusion.1
  71.0 0.1 select_bitcast_fusion
  71.1 0.5 copy.170
  71.6 0.0 collective-permute-done.7
  71.6 0.0 collective-permute-done.6
  71.6 1.9 %collective-permute-start.8 = (f32[3,1,10,1,128]{4,3,2,1,0:T(1,128)S(1)}, f32[3,1,10,1,128]{4,3,2,1,0:T(1,128)S(1)}, u32[]{:S(2)}, u32[]{:S(2)}) collective-permute-start(f32[3,1,10,1,128]{4,3,2,1,0:T(1,128)S(1)} %get-tuple-element.18), channel_id=1, source_target_pairs={{1,0},{0,1},{3,2},{2,3},{5,4},{4,5},{7,6},{6,7},{9,8},{8,9},{11,10... | collective-permute-start | bytes 46088 | tf_op jit(solution)/shard_map/ppermute | solution.py:17
  73.6 12.1 %collective-permute-start.9 = (f32[3,1,10,1,128]{4,3,2,1,0:T(1,128)S(1)}, f32[3,1,10,1,128]{4,3,2,1,0:T(1,128)S(1)}, u32[]{:S(2)}, u32[]{:S(2)}) collective-permute-start(f32[3,1,10,1,128]{4,3,2,1,0:T(1,128)S(1)} %get-tuple-element.19), channel_id=1, source_target_pairs={{0,1},{1,0},{2,3},{3,2},{4,5},{5,4},{6,7},{7,6},{8,9},{9,8},{10,11... | collective-permute-start | bytes 46088 | tf_op jit(solution)/shard_map/ppermute | solution.py:16
  85.7 0.0 copy-start.4
  85.7 0.0 collective-permute-done.11
  85.7 0.2 copy.171
  85.9 0.0 collective-permute-done.8
  85.9 1.0 %collective-permute-done.9 = f32[3,1,10,1,128]{4,3,2,1,0:T(1,128)S(1)} collective-permute-done((f32[3,1,10,1,128]{4,3,2,1,0:T(1,128)S(1)}, f32[3,1,10,1,128]{4,3,2,1,0:T(1,128)S(1)}, u32[]{:S(2)}, u32[]{:S(2)}) %collective-permute-start.9) | collective-permute-done | bytes 15392 | tf_op jit(solution)/shard_map/ppermute | solution.py:16
  87.0 0.0 copy-done.4
  87.0 0.8 fusion.20
  87.8 0.2 copy.183
  88.0 0.2 copy.182
  88.3 0.1 add_bitcast_fusion
  88.3 0.8 copy.177
  (10 shorter events, 0.1 us)
Async XLA Ops:
  1.4 26.9 %collective-permute-start = (f32[3,1,1,8,128]{4,3,2,1,0:T(8,128)S(1)}, f32[3,1,1,8,128]{4,3,2,1,0:T(8,128)S(1)}, u32[]{:S(2)}, u32[]{:S(2)}) collective-permute-start(f32[3,1,1,8,128]{4,3,2,1,0:T(8,128)S(1)} %get-tuple-element.30), channel_id=1, source_target_pairs={{2,0},{4,2},{6,4},{8,6},{10,8},{12,10},{14,12},{16,14},{18,16},{20... | collective-permute-start | bytes 36872 | tf_op jit(solution)/shard_map/ppermute | solution.py:17
  9.5 18.8 %collective-permute-start.1 = (f32[3,1,1,8,128]{4,3,2,1,0:T(8,128)S(1)}, f32[3,1,1,8,128]{4,3,2,1,0:T(8,128)S(1)}, u32[]{:S(2)}, u32[]{:S(2)}) collective-permute-start(f32[3,1,1,8,128]{4,3,2,1,0:T(8,128)S(1)} %get-tuple-element.31), channel_id=1, source_target_pairs={{0,2},{2,4},{4,6},{6,8},{8,10},{10,12},{12,14},{14,16},{16,18},{18... | collective-permute-start | bytes 36872 | tf_op jit(solution)/shard_map/ppermute | solution.py:16
  12.4 5.1 %copy-start.5 = (s32[1,8,8]{2,1,0:T(8,128)S(1)}, s32[1,8,8]{2,1,0:T(8,128)}, u32[]{:S(2)}) copy-start(s32[1,8,8]{2,1,0:T(8,128)} %param.15) | copy-start | bytes 772
  12.6 11.9 %collective-permute-start.4 = (f32[3,1,8,8]{3,2,0,1:T(8,128)S(1)}, f32[3,1,8,8]{3,2,0,1:T(8,128)S(1)}, u32[]{:S(2)}, u32[]{:S(2)}) collective-permute-start(f32[3,1,8,8]{3,2,0,1:T(8,128)S(1)} %bitcast.55), channel_id=1, source_target_pairs={{0,64},{64,128},{128,192},{192,256},{256,320},{320,384},{384,448},... | collective-permute-start | bytes 2312 | tf_op jit(solution)/shard_map/ppermute | solution.py:25
  25.2 0.9 %copy-start = (f32[3,1,8,8,128]{4,3,2,1,0:T(8,128)S(1)}, f32[3,1,8,8,128]{4,3,2,1,0:T(8,128)}, u32[]{:S(2)}) copy-start(f32[3,1,8,8,128]{4,3,2,1,0:T(8,128)} %param.9) | copy-start | bytes 294916
  26.2 17.0 %collective-permute-start.5 = (f32[3,1,8,8]{3,2,0,1:T(8,128)S(1)}, f32[3,1,8,8]{3,2,0,1:T(8,128)S(1)}, u32[]{:S(2)}, u32[]{:S(2)}) collective-permute-start(f32[3,1,8,8]{3,2,0,1:T(8,128)S(1)} %bitcast.50), channel_id=1, source_target_pairs={{64,0},{128,64},{192,128},{256,192},{320,256},{384,320},{448,384},... | collective-permute-start | bytes 2312 | tf_op jit(solution)/shard_map/ppermute | solution.py:25
  28.4 15.0 %collective-permute-start.2 = (f32[3,1,10,1,128]{4,3,2,1,0:T(1,128)S(1)}, f32[3,1,10,1,128]{4,3,2,1,0:T(1,128)S(1)}, u32[]{:S(2)}, u32[]{:S(2)}) collective-permute-start(f32[3,1,10,1,128]{4,3,2,1,0:T(1,128)S(1)} %get-tuple-element.20), channel_id=1, source_target_pairs={{1,0},{0,1},{3,2},{2,3},{5,4},{4,5},{7,6},{6,7},{9,8},{8,9},{11,10... | collective-permute-start | bytes 46088 | tf_op jit(solution)/shard_map/ppermute | solution.py:17
  40.2 13.3 %collective-permute-start.3 = (f32[3,1,10,1,128]{4,3,2,1,0:T(1,128)S(1)}, f32[3,1,10,1,128]{4,3,2,1,0:T(1,128)S(1)}, u32[]{:S(2)}, u32[]{:S(2)}) collective-permute-start(f32[3,1,10,1,128]{4,3,2,1,0:T(1,128)S(1)} %get-tuple-element.21), channel_id=1, source_target_pairs={{0,1},{1,0},{2,3},{3,2},{4,5},{5,4},{6,7},{7,6},{8,9},{9,8},{10,11... | collective-permute-start | bytes 46088 | tf_op jit(solution)/shard_map/ppermute | solution.py:16
  42.4 11.1 %copy-start.2 = (bf16[2,3,1,8,8,128]{5,4,3,2,1,0:T(8,128)(2,1)S(1)}, bf16[2,3,1,8,8,128]{5,4,3,2,1,0:T(8,128)(2,1)}, u32[]{:S(2)}) copy-start(bf16[2,3,1,8,8,128]{5,4,3,2,1,0:T(8,128)(2,1)} %param.12) | copy-start | bytes 294916
  42.4 11.1 %copy-start.3 = (f32[3,1,8,8,128]{4,3,2,1,0:T(8,128)S(1)}, f32[3,1,8,8,128]{4,3,2,1,0:T(8,128)}, u32[]{:S(2)}) copy-start(f32[3,1,8,8,128]{4,3,2,1,0:T(8,128)} %param.10) | copy-start | bytes 294916
  43.1 10.4 %copy-start.1 = (f32[1,8,8,128]{3,2,1,0:T(8,128)S(1)}, f32[1,8,8,128]{3,2,1,0:T(8,128)}, u32[]{:S(2)}) copy-start(f32[1,8,8,128]{3,2,1,0:T(8,128)} %param.11) | copy-start | bytes 98308
  53.9 16.3 %collective-permute-start.10 = (f32[3,1,8,8]{3,2,0,1:T(8,128)S(1)}, f32[3,1,8,8]{3,2,0,1:T(8,128)S(1)}, u32[]{:S(2)}, u32[]{:S(2)}) collective-permute-start(f32[3,1,8,8]{3,2,0,1:T(8,128)S(1)} %bitcast.54), channel_id=1, source_target_pairs={{0,64},{64,128},{128,192},{192,256},{256,320},{320,384},{384,448},... | collective-permute-start | bytes 2312 | tf_op jit(solution)/shard_map/ppermute | solution.py:25
  59.4 12.2 %collective-permute-start.7 = (f32[3,1,1,8,128]{4,3,2,1,0:T(8,128)S(1)}, f32[3,1,1,8,128]{4,3,2,1,0:T(8,128)S(1)}, u32[]{:S(2)}, u32[]{:S(2)}) collective-permute-start(f32[3,1,1,8,128]{4,3,2,1,0:T(8,128)S(1)} %get-tuple-element.22), channel_id=1, source_target_pairs={{0,2},{2,4},{4,6},{6,8},{8,10},{10,12},{12,14},{14,16},{16,18},{18... | collective-permute-start | bytes 36872 | tf_op jit(solution)/shard_map/ppermute | solution.py:16
  61.4 10.2 %collective-permute-start.6 = (f32[3,1,1,8,128]{4,3,2,1,0:T(8,128)S(1)}, f32[3,1,1,8,128]{4,3,2,1,0:T(8,128)S(1)}, u32[]{:S(2)}, u32[]{:S(2)}) collective-permute-start(f32[3,1,1,8,128]{4,3,2,1,0:T(8,128)S(1)} %get-tuple-element.23), channel_id=1, source_target_pairs={{2,0},{4,2},{6,4},{8,6},{10,8},{12,10},{14,12},{16,14},{18,16},{20... | collective-permute-start | bytes 36872 | tf_op jit(solution)/shard_map/ppermute | solution.py:17
  68.3 17.4 %collective-permute-start.11 = (f32[3,1,8,8]{3,2,0,1:T(8,128)S(1)}, f32[3,1,8,8]{3,2,0,1:T(8,128)S(1)}, u32[]{:S(2)}, u32[]{:S(2)}) collective-permute-start(f32[3,1,8,8]{3,2,0,1:T(8,128)S(1)} %bitcast.51), channel_id=1, source_target_pairs={{64,0},{128,64},{192,128},{256,192},{320,256},{384,320},{448,384},... | collective-permute-start | bytes 2312 | tf_op jit(solution)/shard_map/ppermute | solution.py:25
  71.6 14.3 %collective-permute-start.8 = (f32[3,1,10,1,128]{4,3,2,1,0:T(1,128)S(1)}, f32[3,1,10,1,128]{4,3,2,1,0:T(1,128)S(1)}, u32[]{:S(2)}, u32[]{:S(2)}) collective-permute-start(f32[3,1,10,1,128]{4,3,2,1,0:T(1,128)S(1)} %get-tuple-element.18), channel_id=1, source_target_pairs={{1,0},{0,1},{3,2},{2,3},{5,4},{4,5},{7,6},{6,7},{9,8},{8,9},{11,10... | collective-permute-start | bytes 46088 | tf_op jit(solution)/shard_map/ppermute | solution.py:17
  73.6 13.4 %collective-permute-start.9 = (f32[3,1,10,1,128]{4,3,2,1,0:T(1,128)S(1)}, f32[3,1,10,1,128]{4,3,2,1,0:T(1,128)S(1)}, u32[]{:S(2)}, u32[]{:S(2)}) collective-permute-start(f32[3,1,10,1,128]{4,3,2,1,0:T(1,128)S(1)} %get-tuple-element.19), channel_id=1, source_target_pairs={{0,1},{1,0},{2,3},{3,2},{4,5},{5,4},{6,7},{7,6},{8,9},{9,8},{10,11... | collective-permute-start | bytes 46088 | tf_op jit(solution)/shard_map/ppermute | solution.py:16
  85.7 1.3 %copy-start.4 = (bf16[2,3,1,8,8,128]{5,4,3,2,1,0:T(8,128)(2,1)S(1)}, bf16[2,3,1,8,8,128]{5,4,3,2,1,0:T(8,128)(2,1)}, u32[]{:S(2)}) copy-start(bf16[2,3,1,8,8,128]{5,4,3,2,1,0:T(8,128)(2,1)} %param.13) | copy-start | bytes 294916
where the time goes:
time: 89.7 us; the launch traced here: 89.1 us
  starting transfers between devices  61.2 us (68%)
  waiting for transfers between devices  18.1 us (20%)
  local copies, waits for them, and re-layouts  6.9 us (8%)
  between operations  1.63 us (2%)
  other arithmetic  1.3 us (1%)
    ppermute x4, starting transfers between devices, with_halo(): after = lax.ppermute(initial, axis, down)  28.8 us
    ppermute x4, starting transfers between devices, with_halo(): before = lax.ppermute(last, axis, up)  18.1 us
    ppermute x4, starting transfers between devices, shifted(): return lax.ppermute(value, axis, pairs)  14.3 us
    ppermute x4, waiting for transfers between devices, with_halo(): before = lax.ppermute(last, axis, up)  11.2 us
    ppermute x4, waiting for transfers between devices, shifted(): return lax.ppermute(value, axis, pairs)  6.9 us
    unnamed x18, local copies, waits for them, and re-layouts  1.82 us
  transfers between devices with their start and end apart: 12, of which 3 were waited for; matrix products, arithmetic and copies ran while one was open for 5% of the time, Pallas kernels for 0%

commit v1 on v0

v1 whole, which is shorter than its diff:
```python
import jax
import jax.numpy as jnp
from jax import lax
from jax.sharding import PartitionSpec as P

STEPS = 2


def ring(axis, by):
    peers = lax.axis_size(axis)
    return [(i, (i + by) % peers) for i in range(peers)]


def open_chain(axis, by):
    peers = lax.axis_size(axis)
    return [(i, i + by) for i in range(peers) if 0 <= i + by < peers]


def exchange(field):
    x_before = lax.ppermute(field[:, :, -1:], "patch", ring("patch", 1))
    x_after = lax.ppermute(field[:, :, :1], "patch", ring("patch", -1))
    peers = lax.axis_size("cross")
    if peers == 1:
        y_before = field[:, :, :, -1:]
        y_after = field[:, :, :, :1]
    elif peers == 2:
        edges = jnp.concatenate([field[:, :, :, :1], field[:, :, :, -1:]], axis=3)
        got = lax.ppermute(edges, "cross", [(0, 1), (1, 0)])
        y_before = got[:, :, :, 1:2]
        y_after = got[:, :, :, 0:1]
    else:
        y_before = lax.ppermute(field[:, :, :, -1:], "cross", ring("cross", 1))
        y_after = lax.ppermute(field[:, :, :, :1], "cross", ring("cross", -1))
    from_above = lax.ppermute(field[:, :, :, :, -1], "grid", open_chain("grid", 1))
    from_below = lax.ppermute(field[:, :, :, :, 0], "grid", open_chain("grid", -1))
    return x_before, x_after, y_before, y_after, from_above, from_below


def local(
    adjoint_now,
    adjoint_prev,
    stiffness,
    adjoint_source,
    forward_field,
    material_mask,
    interface_map,
):
    rows = adjoint_now.shape[2]
    cols = adjoint_now.shape[3]
    flat_map = interface_map.reshape(-1)
    is_top = lax.axis_index("grid") == 0
    patch_mask = material_mask[0, 0, 0].astype(jnp.float32)
    field = adjoint_now
    older = adjoint_prev
    kernel = jnp.zeros(stiffness.shape, jnp.float32)
    for step in range(STEPS):
        slot = STEPS - 1 - step
        x_before, x_after, y_before, y_after, from_above, from_below = exchange(field)
        gathered = jnp.take(from_above.reshape(3, rows * cols), flat_map, axis=1).reshape(
            3, 1, rows, cols
        )
        top_plane = jnp.where(is_top, field[:, :, :, :, 0], gathered)
        upper = jnp.concatenate([top_plane[..., None], field[..., :-1]], axis=4)
        lower = jnp.concatenate([field[..., 1:], from_below[..., None]], axis=4)
        xs = jnp.concatenate([x_before, field, x_after], axis=2)
        ys = jnp.concatenate([y_before, field, y_after], axis=3)
        side = xs[:, :, 2:] + xs[:, :, :-2]
        side = side + ys[:, :, :, 2:] + ys[:, :, :, :-2]
        lap = side + upper + lower - 6.0 * field
        fresh = (
            2.0 * field - older + stiffness * lap + adjoint_source[slot].astype(jnp.float32)
        ) * patch_mask
        kernel = kernel + jnp.sum(fresh * forward_field[slot].astype(jnp.float32), axis=0)
        older = field
        field = fresh
    return (field, kernel)


def solution(mesh):
    in_specs = (
        P(None, "grid", "patch", "cross", None),
        P(None, "grid", "patch", "cross", None),
        P("grid", "patch", "cross", None),
        P(None, None, "grid", "patch", "cross", None),
        P(None, None, "grid", "patch", "cross", None),
        P("grid", "patch", "cross"),
        P("grid", "patch", "cross"),
    )
    out_specs = (P(None, "grid", "patch", "cross", None), P("grid", "patch", "cross", None))
    return jax.shard_map(local, mesh=mesh, in_specs=in_specs, out_specs=out_specs, check_vma=False)
```

time: 89.7 us -> 72.7 us (0.81)
  waiting for transfers between devices: 18.1 us -> 7.43 us
  starting transfers between devices: 61.2 us -> 54.4 us
    ppermute x12 -> x10, waiting for transfers between devices: 18.1 us -> 7.43 us  [the longest x2 6.56 us: exchange(): got = lax.ppermute(edges, 'cross', [(0, 1), (1, 0)])]
    ppermute x12 -> x10, starting transfers between devices: 61.2 us -> 54.4 us  [the longest x2 24.2 us: exchange(): got = lax.ppermute(edges, 'cross', [(0, 1), (1, 0)])]
    unnamed x18 -> x16, local copies, waits for them, and re-layouts: 1.82 us -> 2.23 us
  transfers between devices with their start and end apart: 12 -> 10, of which waited for: 3 -> 2; matrix products, arithmetic and copies ran while one was open for 5% -> 6% of each run, Pallas kernels for 0% -> 0%
where the time goes in v1:
time: 72.7 us; the launch traced here: 72.2 us
  starting transfers between devices  54.4 us (75%)
  local copies, waits for them, and re-layouts  7.5 us (10%)
  waiting for transfers between devices  7.43 us (10%)
  between operations  1.59 us (2%)
  other arithmetic  1.21 us (2%)
    ppermute x2, starting transfers between devices, exchange(): got = lax.ppermute(edges, 'cross', [(0, 1), (1, 0)])  24.2 us
    ppermute x2, starting transfers between devices, exchange(): x_after = lax.ppermute(field[:, :, :1], 'patch', ring('patch', -1))  15.1 us
    ppermute x2, starting transfers between devices, exchange(): lax.ppermute(field[:, :, :, :, -1], 'grid', open_chain('grid', 1))  7.46 us
    ppermute x2, waiting for transfers between devices, exchange(): got = lax.ppermute(edges, 'cross', [(0, 1), (1, 0)])  6.56 us
    ppermute x2, starting transfers between devices, exchange(): x_before = lax.ppermute(field[:, :, -1:], 'patch', ring('patch', 1))  3.84 us
    ppermute x2, starting transfers between devices, exchange(): lax.ppermute(field[:, :, :, :, 0], 'grid', open_chain('grid', -1))  3.84 us
    unnamed x16, local copies, waits for them, and re-layouts  2.23 us
  transfers between devices with their start and end apart: 10, of which 2 were waited for; matrix products, arithmetic and copies ran while one was open for 6% of the time, Pallas kernels for 0%

profile of v1, /device:TPU:1, one launch (start us, length us, event | category | flops | bytes accessed | tf_op | source)
XLA Modules:
  0.0 72.2 jit_solution(16165538725521884569)
XLA Ops:
  0.6 0.0 copy-start
  0.6 0.8 %fusion.27 = (f32[3,1,1,8,128]{4,3,2,1,0:T(8,128)S(1)}, f32[3,1,1,8,128]{4,3,2,1,0:T(8,128)S(1)}) fusion(f32[3,1,8,8,128]{4,3,2,1,0:T(8,128)} %param.9), kind=kLoop, calls=%fused_computation.55 | loop fusion | bytes 49152 | tf_op jit(solution)/shard_map/slice | solution.py:21
  1.4 8.1 %collective-permute-start = (f32[3,1,1,8,128]{4,3,2,1,0:T(8,128)S(1)}, f32[3,1,1,8,128]{4,3,2,1,0:T(8,128)S(1)}, u32[]{:S(2)}, u32[]{:S(2)}) collective-permute-start(f32[3,1,1,8,128]{4,3,2,1,0:T(8,128)S(1)} %get-tuple-element.28), channel_id=1, source_target_pairs={{0,62},{2,0},{4,2},{6,4},{8,6},{10,8},{12,10},{14,12},{16,14},{18,... | collective-permute-start | bytes 36872 | tf_op jit(solution)/shard_map/ppermute | solution.py:21
  9.5 1.9 %collective-permute-start.1 = (f32[3,1,1,8,128]{4,3,2,1,0:T(8,128)S(1)}, f32[3,1,1,8,128]{4,3,2,1,0:T(8,128)S(1)}, u32[]{:S(2)}, u32[]{:S(2)}) collective-permute-start(f32[3,1,1,8,128]{4,3,2,1,0:T(8,128)S(1)} %get-tuple-element.29), channel_id=1, source_target_pairs={{0,2},{2,4},{4,6},{6,8},{8,10},{10,12},{12,14},{14,16},{16,18},{18... | collective-permute-start | bytes 36872 | tf_op jit(solution)/shard_map/ppermute | solution.py:20
  11.5 1.0 %fusion.28 = (f32[3,1,8,1,128]{4,3,2,1,0:T(1,128)S(1)}, f32[3,1,8,1,128]{4,3,2,1,0:T(1,128)S(1)}) fusion(f32[3,1,8,8,128]{4,3,2,1,0:T(8,128)} %param.9), kind=kLoop, calls=%fused_computation.56 | loop fusion | bytes 49152 | tf_op jit(solution)/shard_map/slice | solution.py:27
  12.5 19.1 %collective-permute-start.2 = (f32[3,1,8,2,128]{4,2,3,1,0:T(8,128)S(1)}, f32[3,1,8,2,128]{4,2,3,1,0:T(8,128)S(1)}, u32[]{:S(2)}, u32[]{:S(2)}) collective-permute-start(f32[3,1,8,2,128]{4,2,3,1,0:T(8,128)S(1)} %pad_maximum_fusion.8), channel_id=1, source_target_pairs={{0,1},{1,0},{2,3},{3,2},{4,5},{5,4},{6,7},{7,6},{8,9},{9,8},{10,11... | collective-permute-start | bytes 73736 | tf_op jit(solution)/shard_map/ppermute | solution.py:28
  31.5 0.0 copy-done
  31.6 0.1 slice_reduce_fusion.2
  31.7 0.2 copy.185
  31.9 0.0 copy-start.5
  31.9 4.4 %collective-permute-start.3 = (f32[3,1,8,8]{3,2,0,1:T(8,128)S(1)}, f32[3,1,8,8]{3,2,0,1:T(8,128)S(1)}, u32[]{:S(2)}, u32[]{:S(2)}) collective-permute-start(f32[3,1,8,8]{3,2,0,1:T(8,128)S(1)} %bitcast.69), channel_id=1, source_target_pairs={{0,64},{64,128},{128,192},{192,256},{256,320},{320,384},{384,448},... | collective-permute-start | bytes 2312 | tf_op jit(solution)/shard_map/ppermute | solution.py:34
  36.3 1.9 %collective-permute-start.4 = (f32[3,1,8,8]{3,2,0,1:T(8,128)S(1)}, f32[3,1,8,8]{3,2,0,1:T(8,128)S(1)}, u32[]{:S(2)}, u32[]{:S(2)}) collective-permute-start(f32[3,1,8,8]{3,2,0,1:T(8,128)S(1)} %bitcast.66), channel_id=1, source_target_pairs={{64,0},{128,64},{192,128},{256,192},{320,256},{384,320},{448,384},... | collective-permute-start | bytes 2312 | tf_op jit(solution)/shard_map/ppermute | solution.py:35
  38.2 0.0 copy-done.5
  38.2 0.1 reshape.112
  38.3 0.1 fusion.26
  39.1 0.0 collective-permute-done.3
  39.1 0.1 copy.158
  39.2 0.6 gather_fusion
  39.8 0.1 select_bitcast_fusion.1
  39.9 0.5 copy.160
  40.4 0.0 copy-start.4
  40.4 0.0 copy-start.2
  40.4 0.8 %collective-permute-done.4 = f32[3,1,8,8]{3,2,0,1:T(8,128)S(1)} collective-permute-done((f32[3,1,8,8]{3,2,0,1:T(8,128)S(1)}, f32[3,1,8,8]{3,2,0,1:T(8,128)S(1)}, u32[]{:S(2)}, u32[]{:S(2)}) %collective-permute-start.4) | collective-permute-done | bytes 800 | tf_op jit(solution)/shard_map/ppermute | solution.py:35
  41.3 0.2 copy.161
  41.5 0.0 copy-start.1
  41.5 0.0 collective-permute-done.2
  41.5 0.0 collective-permute-done
  41.5 0.0 collective-permute-done.1
  41.5 0.0 copy-done.4
  41.5 0.0 copy-done.2
  41.5 0.7 copy-done.1
  42.3 0.1 fusion.17
  42.4 0.2 slice_reduce_fusion.1
  42.6 0.1 fusion.25
  42.7 7.0 %collective-permute-start.5 = (f32[3,1,1,8,128]{4,3,2,1,0:T(8,128)S(1)}, f32[3,1,1,8,128]{4,3,2,1,0:T(8,128)S(1)}, u32[]{:S(2)}, u32[]{:S(2)}) collective-permute-start(f32[3,1,1,8,128]{4,3,2,1,0:T(8,128)S(1)} %get-tuple-element.18), channel_id=1, source_target_pairs={{0,62},{2,0},{4,2},{6,4},{8,6},{10,8},{12,10},{14,12},{16,14},{18,... | collective-permute-start | bytes 36872 | tf_op jit(solution)/shard_map/ppermute | solution.py:21
  49.7 1.9 %collective-permute-start.6 = (f32[3,1,1,8,128]{4,3,2,1,0:T(8,128)S(1)}, f32[3,1,1,8,128]{4,3,2,1,0:T(8,128)S(1)}, u32[]{:S(2)}, u32[]{:S(2)}) collective-permute-start(f32[3,1,1,8,128]{4,3,2,1,0:T(8,128)S(1)} %get-tuple-element.19), channel_id=1, source_target_pairs={{0,2},{2,4},{4,6},{6,8},{8,10},{10,12},{12,14},{14,16},{16,18},{18... | collective-permute-start | bytes 36872 | tf_op jit(solution)/shard_map/ppermute | solution.py:20
  51.6 3.1 %collective-permute-start.8 = (f32[3,1,8,8]{3,2,0,1:T(8,128)S(1)}, f32[3,1,8,8]{3,2,0,1:T(8,128)S(1)}, u32[]{:S(2)}, u32[]{:S(2)}) collective-permute-start(f32[3,1,8,8]{3,2,0,1:T(8,128)S(1)} %bitcast.70), channel_id=1, source_target_pairs={{0,64},{64,128},{128,192},{192,256},{256,320},{320,384},{384,448},... | collective-permute-start | bytes 2312 | tf_op jit(solution)/shard_map/ppermute | solution.py:34
  54.7 1.9 %collective-permute-start.9 = (f32[3,1,8,8]{3,2,0,1:T(8,128)S(1)}, f32[3,1,8,8]{3,2,0,1:T(8,128)S(1)}, u32[]{:S(2)}, u32[]{:S(2)}) collective-permute-start(f32[3,1,8,8]{3,2,0,1:T(8,128)S(1)} %bitcast.67), channel_id=1, source_target_pairs={{64,0},{128,64},{192,128},{256,192},{320,256},{384,320},{448,384},... | collective-permute-start | bytes 2312 | tf_op jit(solution)/shard_map/ppermute | solution.py:35
  56.7 5.1 %collective-permute-start.7 = (f32[3,1,8,2,128]{4,2,3,1,0:T(8,128)S(1)}, f32[3,1,8,2,128]{4,2,3,1,0:T(8,128)S(1)}, u32[]{:S(2)}, u32[]{:S(2)}) collective-permute-start(f32[3,1,8,2,128]{4,2,3,1,0:T(8,128)S(1)} %pad_maximum_fusion.9), channel_id=1, source_target_pairs={{0,1},{1,0},{2,3},{3,2},{4,5},{5,4},{6,7},{7,6},{8,9},{9,8},{10,11... | collective-permute-start | bytes 73736 | tf_op jit(solution)/shard_map/ppermute | solution.py:28
  61.8 0.0 collective-permute-done.8
  61.8 0.1 copy.167
  61.9 0.6 gather_fusion.1
  62.5 0.1 select_bitcast_fusion
  62.6 0.5 copy.169
  63.2 0.0 copy-start.3
  63.2 0.0 collective-permute-done.9
  63.2 0.2 copy.170
  63.4 6.6 %collective-permute-done.7 = f32[3,1,8,2,128]{4,2,3,1,0:T(8,128)S(1)} collective-permute-done((f32[3,1,8,2,128]{4,2,3,1,0:T(8,128)S(1)}, f32[3,1,8,2,128]{4,2,3,1,0:T(8,128)S(1)}, u32[]{:S(2)}, u32[]{:S(2)}) %collective-permute-start.7) | collective-permute-done | bytes 24608 | tf_op jit(solution)/shard_map/ppermute | solution.py:28
  70.0 0.0 collective-permute-done.5
  70.0 0.0 collective-permute-done.6
  70.0 0.0 copy-done.3
  70.0 0.8 %fusion.20 = (f32[8,8,128]{2,1,0:T(8,128)S(1)}, f32[8,8,128]{2,1,0:T(8,128)S(1)}, f32[3,1,8,8,128]{4,3,2,1,0:T(8,128)}) fusion(bf16[2,3,1,8,8,128]{5,4,3,1,2,0:T(8,128)(2,1)S(1)} %bitcast.55, f32[3,1,8,8,128]{4,3,2,1,0:T(8,128)S(1)} %fusion.17, f32[]{:T(128)} %bitcast.10, bf16[2,3,1,8,8,128]{5,4,3,1,2,0:T(8,128)(2,1)S(1)} %bitcast.54, ...), kind=kLoop, calls=%fused_computation.33 | loop fusion | flops 622592 | bytes 786436 | tf_op jit(solution)/shard_map/reduce_sum | solution.py:73
  70.8 0.2 copy.182
  71.0 0.2 copy.181
  71.3 0.1 add_bitcast_fusion
  71.3 0.8 %copy.176 = f32[1,8,8,128]{3,2,1,0:T(8,128)} copy(f32[1,8,8,128]{2,1,3,0:T(8,128)S(1)} %add_bitcast_fusion) | data formatting | bytes 65536
  (11 shorter events, 0.1 us)
Async XLA Ops:
  0.6 30.9 %copy-start = (f32[3,1,8,8,128]{4,3,2,1,0:T(8,128)S(1)}, f32[3,1,8,8,128]{4,3,2,1,0:T(8,128)}, u32[]{:S(2)}) copy-start(f32[3,1,8,8,128]{4,3,2,1,0:T(8,128)} %param.9) | copy-start | bytes 294916
  1.4 40.1 %collective-permute-start = (f32[3,1,1,8,128]{4,3,2,1,0:T(8,128)S(1)}, f32[3,1,1,8,128]{4,3,2,1,0:T(8,128)S(1)}, u32[]{:S(2)}, u32[]{:S(2)}) collective-permute-start(f32[3,1,1,8,128]{4,3,2,1,0:T(8,128)S(1)} %get-tuple-element.28), channel_id=1, source_target_pairs={{0,62},{2,0},{4,2},{6,4},{8,6},{10,8},{12,10},{14,12},{16,14},{18,... | collective-permute-start | bytes 36872 | tf_op jit(solution)/shard_map/ppermute | solution.py:21
  9.5 32.0 %collective-permute-start.1 = (f32[3,1,1,8,128]{4,3,2,1,0:T(8,128)S(1)}, f32[3,1,1,8,128]{4,3,2,1,0:T(8,128)S(1)}, u32[]{:S(2)}, u32[]{:S(2)}) collective-permute-start(f32[3,1,1,8,128]{4,3,2,1,0:T(8,128)S(1)} %get-tuple-element.29), channel_id=1, source_target_pairs={{0,2},{2,4},{4,6},{6,8},{8,10},{10,12},{12,14},{14,16},{16,18},{18... | collective-permute-start | bytes 36872 | tf_op jit(solution)/shard_map/ppermute | solution.py:20
  12.5 29.0 %collective-permute-start.2 = (f32[3,1,8,2,128]{4,2,3,1,0:T(8,128)S(1)}, f32[3,1,8,2,128]{4,2,3,1,0:T(8,128)S(1)}, u32[]{:S(2)}, u32[]{:S(2)}) collective-permute-start(f32[3,1,8,2,128]{4,2,3,1,0:T(8,128)S(1)} %pad_maximum_fusion.8), channel_id=1, source_target_pairs={{0,1},{1,0},{2,3},{3,2},{4,5},{5,4},{6,7},{7,6},{8,9},{9,8},{10,11... | collective-permute-start | bytes 73736 | tf_op jit(solution)/shard_map/ppermute | solution.py:28
  31.9 6.3 %copy-start.5 = (s32[1,8,8]{2,1,0:T(8,128)S(1)}, s32[1,8,8]{2,1,0:T(8,128)}, u32[]{:S(2)}) copy-start(s32[1,8,8]{2,1,0:T(8,128)} %param.15) | copy-start | bytes 772
  31.9 7.2 %collective-permute-start.3 = (f32[3,1,8,8]{3,2,0,1:T(8,128)S(1)}, f32[3,1,8,8]{3,2,0,1:T(8,128)S(1)}, u32[]{:S(2)}, u32[]{:S(2)}) collective-permute-start(f32[3,1,8,8]{3,2,0,1:T(8,128)S(1)} %bitcast.69), channel_id=1, source_target_pairs={{0,64},{64,128},{128,192},{192,256},{256,320},{320,384},{384,448},... | collective-permute-start | bytes 2312 | tf_op jit(solution)/shard_map/ppermute | solution.py:34
  36.3 5.0 %collective-permute-start.4 = (f32[3,1,8,8]{3,2,0,1:T(8,128)S(1)}, f32[3,1,8,8]{3,2,0,1:T(8,128)S(1)}, u32[]{:S(2)}, u32[]{:S(2)}) collective-permute-start(f32[3,1,8,8]{3,2,0,1:T(8,128)S(1)} %bitcast.66), channel_id=1, source_target_pairs={{64,0},{128,64},{192,128},{256,192},{320,256},{384,320},{448,384},... | collective-permute-start | bytes 2312 | tf_op jit(solution)/shard_map/ppermute | solution.py:35
  40.4 1.1 %copy-start.4 = (f32[3,1,8,8,128]{4,3,2,1,0:T(8,128)S(1)}, f32[3,1,8,8,128]{4,3,2,1,0:T(8,128)}, u32[]{:S(2)}) copy-start(f32[3,1,8,8,128]{4,3,2,1,0:T(8,128)} %param.10) | copy-start | bytes 294916
  40.4 1.1 %copy-start.2 = (bf16[2,3,1,8,8,128]{5,4,3,2,1,0:T(8,128)(2,1)S(1)}, bf16[2,3,1,8,8,128]{5,4,3,2,1,0:T(8,128)(2,1)}, u32[]{:S(2)}) copy-start(bf16[2,3,1,8,8,128]{5,4,3,2,1,0:T(8,128)(2,1)} %param.12) | copy-start | bytes 294916
  41.5 0.8 %copy-start.1 = (f32[1,8,8,128]{3,2,1,0:T(8,128)S(1)}, f32[1,8,8,128]{3,2,1,0:T(8,128)}, u32[]{:S(2)}) copy-start(f32[1,8,8,128]{3,2,1,0:T(8,128)} %param.11) | copy-start | bytes 98308
  42.7 27.3 %collective-permute-start.5 = (f32[3,1,1,8,128]{4,3,2,1,0:T(8,128)S(1)}, f32[3,1,1,8,128]{4,3,2,1,0:T(8,128)S(1)}, u32[]{:S(2)}, u32[]{:S(2)}) collective-permute-start(f32[3,1,1,8,128]{4,3,2,1,0:T(8,128)S(1)} %get-tuple-element.18), channel_id=1, source_target_pairs={{0,62},{2,0},{4,2},{6,4},{8,6},{10,8},{12,10},{14,12},{16,14},{18,... | collective-permute-start | bytes 36872 | tf_op jit(solution)/shard_map/ppermute | solution.py:21
  49.7 20.3 %collective-permute-start.6 = (f32[3,1,1,8,128]{4,3,2,1,0:T(8,128)S(1)}, f32[3,1,1,8,128]{4,3,2,1,0:T(8,128)S(1)}, u32[]{:S(2)}, u32[]{:S(2)}) collective-permute-start(f32[3,1,1,8,128]{4,3,2,1,0:T(8,128)S(1)} %get-tuple-element.19), channel_id=1, source_target_pairs={{0,2},{2,4},{4,6},{6,8},{8,10},{10,12},{12,14},{14,16},{16,18},{18... | collective-permute-start | bytes 36872 | tf_op jit(solution)/shard_map/ppermute | solution.py:20
  51.6 10.2 %collective-permute-start.8 = (f32[3,1,8,8]{3,2,0,1:T(8,128)S(1)}, f32[3,1,8,8]{3,2,0,1:T(8,128)S(1)}, u32[]{:S(2)}, u32[]{:S(2)}) collective-permute-start(f32[3,1,8,8]{3,2,0,1:T(8,128)S(1)} %bitcast.70), channel_id=1, source_target_pairs={{0,64},{64,128},{128,192},{192,256},{256,320},{320,384},{384,448},... | collective-permute-start | bytes 2312 | tf_op jit(solution)/shard_map/ppermute | solution.py:34
  54.7 8.5 %collective-permute-start.9 = (f32[3,1,8,8]{3,2,0,1:T(8,128)S(1)}, f32[3,1,8,8]{3,2,0,1:T(8,128)S(1)}, u32[]{:S(2)}, u32[]{:S(2)}) collective-permute-start(f32[3,1,8,8]{3,2,0,1:T(8,128)S(1)} %bitcast.67), channel_id=1, source_target_pairs={{64,0},{128,64},{192,128},{256,192},{320,256},{384,320},{448,384},... | collective-permute-start | bytes 2312 | tf_op jit(solution)/shard_map/ppermute | solution.py:35
  56.7 13.3 %collective-permute-start.7 = (f32[3,1,8,2,128]{4,2,3,1,0:T(8,128)S(1)}, f32[3,1,8,2,128]{4,2,3,1,0:T(8,128)S(1)}, u32[]{:S(2)}, u32[]{:S(2)}) collective-permute-start(f32[3,1,8,2,128]{4,2,3,1,0:T(8,128)S(1)} %pad_maximum_fusion.9), channel_id=1, source_target_pairs={{0,1},{1,0},{2,3},{3,2},{4,5},{5,4},{6,7},{7,6},{8,9},{9,8},{10,11... | collective-permute-start | bytes 73736 | tf_op jit(solution)/shard_map/ppermute | solution.py:28
  63.2 6.8 %copy-start.3 = (bf16[2,3,1,8,8,128]{5,4,3,2,1,0:T(8,128)(2,1)S(1)}, bf16[2,3,1,8,8,128]{5,4,3,2,1,0:T(8,128)(2,1)}, u32[]{:S(2)}) copy-start(bf16[2,3,1,8,8,128]{5,4,3,2,1,0:T(8,128)(2,1)} %param.13) | copy-start | bytes 294916
